TPU v7x, 256 devices: a whole 4x4x8 slice. The times are simulated.
256 devices in a mesh: tile: 16 (over z, core), tensor: 16 (over y, x).
Axes of the slice: x: 4, y: 4, z: 8, core: 2. Of those that a mesh axis runs over, the one named last changes fastest.
Arguments:
- image_hidden: bfloat16 [8, 32, 32, 3072], P(None, 'tile', 'tensor'), may hold values from -6 to 6
- text_hidden: bfloat16 [8, 512, 3072], P(None, ('tile', 'tensor')), may hold values from -6 to 6
- latents: float32 [8, 32, 2048], P(None, 'tile', 'tensor'), may hold values from -6 to 6
- step_index: int32 [8], replicated, may hold values from 0 to 27
- anchor: int32 [8, 2], replicated, may hold values from 0 to 63
- text_len: int32 [8], replicated, may hold values from 64 to 512
- mod_image: float32 [8, 3, 3072], replicated, may hold values from -3 to 3
- mod_text: float32 [8, 3, 3072], replicated, may hold values from -3 to 3
- mod_mlp: float32 [8, 3, 3072], replicated, may hold values from -3 to 3
- mod_final: float32 [8, 2, 3072], replicated, may hold values from -3 to 3
- qkv_image: bfloat16 [3072, 3, 2048], P(None, None, 'tensor'), may hold values from -0.109375 to 0.109375
- qkv_text: bfloat16 [3072, 3, 2048], P(None, None, 'tensor'), may hold values from -0.109375 to 0.109375
- proj_image: bfloat16 [2048, 3072], P('tensor'), may hold values from -0.125 to 0.125
- proj_text: bfloat16 [2048, 3072], P('tensor'), may hold values from -0.125 to 0.125
- qk_gain: float32 [2, 2, 128], replicated, may hold values from 0.5 to 10
- mlp_expand: bfloat16 [3072, 6144], P(None, 'tensor'), may hold values from -0.109375 to 0.109375
- mlp_reduce: bfloat16 [6144, 3072], P('tensor'), may hold values from -0.078125 to 0.078125
- final_weight: bfloat16 [3072, 64], replicated, may hold values from -0.109375 to 0.109375
Outputs:
- image_out: bfloat16 [8, 32, 32, 3072], P(None, 'tile', 'tensor')
- text_out: bfloat16 [8, 512, 3072], P(None, ('tile', 'tensor'))
- latents_ext: float32 [8, 64, 2048], P(None, 'tile', 'tensor')
Inputs may be any that keep to these rules, and one draw needn't show every extreme that they name: text_len gives each request's live text tokens; slots at or past it take no part as keys. step_index is a step of the 28-step plan.
All inputs are finite; a program needn't handle non-finite values.
Results may differ from a plain program's by a relative error of at most 0.0085.
The roundings to bfloat16 on the way count: a program that leaves them out, or rounds other values in their place, can miss the bound.
Values may be sent and summed in bfloat16 or wider, within the bound.
No kernel may reach another device: no remote copies, remote signals or barrier semaphores. Data moves between devices by JAX's collectives and lax.ppermute only.
A program may use at most 128 MiB of HBM per device.

v0:
```python
import math
import jax
import jax.numpy as jnp
from jax import lax
from jax.sharding import PartitionSpec as P

HEAD_DIM = 128
GRID = 32
NSTEPS = 28
norm_eps = 1e-06
time_shift = 3.0


def padded(value, sides, width):
    for axis, dim in sides:
        size, length = (lax.axis_size(axis), value.shape[dim])
        up = [(i, (i + 1) % size) for i in range(size - 1)]
        down = [(j, i) for i, j in up]
        last = lax.slice_in_dim(value, length - width, length, axis=dim)
        leading = lax.slice_in_dim(value, 0, width, axis=dim)
        before = lax.ppermute(last, axis, up)
        after = lax.ppermute(leading, axis, down)
        value = jnp.concatenate([before, value, after], axis=dim)
    return value


def layer_norm(values):
    average = jnp.mean(values, -1, keepdims=True)
    centred = values - average
    spread = jnp.mean(centred * centred, -1, keepdims=True)
    return centred * lax.rsqrt(spread + norm_eps)


def modulate(hidden, shift, stretch):
    normed = layer_norm(hidden.astype(jnp.float32))
    return ((1.0 + stretch) * normed + shift).astype(jnp.bfloat16)


def rope_tables(row_ids, col_ids):
    lane = jnp.arange(2 * 64, dtype=jnp.int32)
    pair_index = lane // 2
    row_rank = (pair_index - 8).astype(jnp.float32)
    col_rank = (pair_index - 36).astype(jnp.float32)
    log_base = math.log(10000.0)
    row_freq = jnp.where(
        (pair_index >= 8) & (pair_index < 36), jnp.exp(-2.0 * row_rank / 56.0 * log_base), 0.0
    )
    col_freq = jnp.where(pair_index >= 36, jnp.exp(-2.0 * col_rank / 56.0 * log_base), 0.0)
    angles = row_ids[..., None] * row_freq + col_ids[..., None] * col_freq
    sign_table = jnp.where(lane % 2 == 0, -1.0, 1.0).astype(jnp.float32)
    return (jnp.cos(angles), jnp.sin(angles) * sign_table)


def rotate(values, cos_table, sin_table):
    lane = lax.broadcasted_iota(jnp.int32, values.shape, values.ndim - 1)
    swapped = jnp.where(lane % 2 == 0, jnp.roll(values, -1, axis=-1), jnp.roll(values, 1, axis=-1))
    return values * cos_table + swapped * sin_table


def head_norm(projected, head_gain):
    squares = jnp.mean(projected * projected, -1, keepdims=True)
    return projected * lax.rsqrt(squares + norm_eps) * head_gain


def sigma_of(step_float):
    level = 1.0 - step_float / NSTEPS
    return time_shift * level / (1.0 + (time_shift - 1.0) * level)


def key_usable(text_len, key_count, text_tile, block_len):
    key_pos = jnp.arange(key_count, dtype=jnp.int32)
    owner_tile = key_pos // block_len
    offset = key_pos % block_len
    text_pos = owner_tile * text_tile + offset
    return jnp.logical_or(offset[None, :] >= text_tile, text_pos[None, :] < text_len[:, None])


def sum_over_tensor(term, owners, narrow):
    if not narrow:
        return lax.psum_scatter(term, "tensor", scatter_dimension=0, tiled=True)
    parts = term.astype(jnp.bfloat16).reshape((owners, -1) + term.shape[1:])
    parts = lax.all_to_all(parts, "tensor", 0, 0, tiled=True)
    return jnp.sum(parts.astype(jnp.float32), 0)


NARROW_SUMS = True


def per_device(
    image_hidden,
    text_hidden,
    latents,
    step_index,
    anchor,
    text_len,
    mod_image,
    mod_text,
    mod_mlp,
    mod_final,
    qkv_image,
    qkv_text,
    proj_image,
    proj_text,
    qk_gain,
    mlp_expand,
    mlp_reduce,
    final_weight,
):
    requests, tile_rows, tile_cols, model_width = image_hidden.shape
    local_cols = qkv_image.shape[2]
    local_heads = local_cols // HEAD_DIM
    owners = lax.axis_size("tensor")
    own_image = tile_rows * tile_cols
    own_text = text_hidden.shape[1]
    slots = own_image + own_text
    image_own = image_hidden.reshape(requests, own_image, model_width).transpose(1, 0, 2)
    text_own = text_hidden.transpose(1, 0, 2)
    image_mod_own = modulate(image_own, mod_image[None, :, 0, :], mod_image[None, :, 1, :])
    text_mod_own = modulate(text_own, mod_text[None, :, 0, :], mod_text[None, :, 1, :])
    image_count = owners * own_image
    text_tile = owners * own_text
    block_len = text_tile + image_count
    image_mod = lax.all_gather(image_mod_own, "tensor", axis=0, tiled=True).reshape(
        image_count * requests, model_width
    )
    text_mod = lax.all_to_all(
        jnp.broadcast_to(text_mod_own[None], (owners,) + text_mod_own.shape),
        "tensor",
        0,
        0,
        tiled=True,
    ).reshape(text_tile * requests, model_width)
    tile_index = lax.axis_index("tile")
    token_index = jnp.arange(image_count, dtype=jnp.int32)
    owner = token_index // own_image
    within = token_index % own_image
    row_ids = (anchor[None, :, 0] + tile_index * tile_rows + (within // tile_cols)[:, None]).astype(
        jnp.float32
    )
    col_ids = (anchor[None, :, 1] + (owner * tile_cols + within % tile_cols)[:, None]).astype(
        jnp.float32
    )
    cos_table, sin_table = rope_tables(row_ids.reshape(-1), col_ids.reshape(-1))
    cos_table = cos_table[:, None, :]
    sin_table = sin_table[:, None, :]
    image_qkv = jnp.dot(
        image_mod,
        qkv_image.reshape(model_width, 3 * local_cols),
        preferred_element_type=jnp.float32,
    ).reshape(image_count * requests, 3, local_heads, HEAD_DIM)
    text_qkv = jnp.dot(
        text_mod, qkv_text.reshape(model_width, 3 * local_cols), preferred_element_type=jnp.float32
    ).reshape(text_tile * requests, 3, local_heads, HEAD_DIM)
    token_shape = (block_len, requests, local_heads, HEAD_DIM)
    query = jnp.concatenate(
        [
            head_norm(text_qkv[:, 0], qk_gain[1, 0]).astype(jnp.bfloat16),
            rotate(head_norm(image_qkv[:, 0], qk_gain[0, 0]), cos_table, sin_table).astype(
                jnp.bfloat16
            ),
        ],
        0,
    ).reshape(token_shape)
    keys = jnp.concatenate(
        [
            head_norm(text_qkv[:, 1], qk_gain[1, 1]).astype(jnp.bfloat16),
            rotate(head_norm(image_qkv[:, 1], qk_gain[0, 1]), cos_table, sin_table).astype(
                jnp.bfloat16
            ),
        ],
        0,
    ).reshape(token_shape)
    values = (
        jnp.concatenate([text_qkv[:, 2], image_qkv[:, 2]], 0)
        .astype(jnp.bfloat16)
        .reshape(token_shape)
    )
    score_scale = 1.0 / math.sqrt(HEAD_DIM)
    tiles = lax.axis_size("tile")
    parts = tiles // requests
    part_len = block_len // parts
    keys_r = jnp.repeat(keys.transpose(1, 0, 2, 3), parts, axis=0)
    values_r = jnp.repeat(values.transpose(1, 0, 2, 3), parts, axis=0)
    query_r = query.transpose(1, 0, 2, 3).reshape(tiles, part_len, local_heads, HEAD_DIM)
    outgoing = jnp.concatenate([keys_r, values_r, query_r], 1)
    incoming = lax.all_to_all(outgoing, "tile", 0, 0, tiled=True)
    keys_all = incoming[:, :block_len].reshape(tiles * block_len, local_heads, HEAD_DIM)
    values_all = incoming[:, block_len : 2 * block_len].reshape(
        tiles * block_len, local_heads, HEAD_DIM
    )
    query_mine = incoming[:, 2 * block_len :].reshape(tiles * part_len, local_heads, HEAD_DIM)
    my_request = tile_index // parts
    usable = key_usable(text_len[my_request][None], keys_all.shape[0], text_tile, block_len)[0][
        None, None, :
    ]
    scores = (
        jnp.einsum("qhd,khd->hqk", query_mine, keys_all, preferred_element_type=jnp.float32)
        * score_scale
    )
    row_top = jnp.max(jnp.where(usable, scores, -jnp.inf), -1, keepdims=True)
    weights_raw = jnp.where(usable, jnp.exp(scores - row_top), 0.0)
    weight_sum = jnp.sum(weights_raw, -1, keepdims=True)
    accum = jnp.einsum(
        "hqk,khd->hqd",
        weights_raw.astype(jnp.bfloat16),
        values_all,
        preferred_element_type=jnp.float32,
    )
    attended_mine = (
        (accum / weight_sum)
        .astype(jnp.bfloat16)
        .transpose(1, 0, 2)
        .reshape(tiles, part_len, local_heads * HEAD_DIM)
    )
    returned = lax.all_to_all(attended_mine, "tile", 0, 0, tiled=True)
    attended = returned.reshape(requests, block_len, local_cols).transpose(1, 0, 2)
    text_att = attended[:text_tile].reshape(text_tile * requests, local_cols)
    image_att = attended[text_tile:].reshape(image_count * requests, local_cols)
    image_term = jnp.dot(image_att, proj_image, preferred_element_type=jnp.float32).reshape(
        image_count, requests, model_width
    )
    image_sum = sum_over_tensor(image_term, owners, NARROW_SUMS)
    text_term = jnp.dot(text_att, proj_text, preferred_element_type=jnp.float32).reshape(
        text_tile, requests, model_width
    )
    after_image = (image_sum[0, 0, 0] * 0.0).astype(text_term.dtype)
    text_sum = sum_over_tensor(text_term + after_image, owners, NARROW_SUMS)
    image_mid = (image_own.astype(jnp.float32) + mod_image[None, :, 2, :] * image_sum).astype(
        jnp.bfloat16
    )
    mlp_mod = modulate(image_mid, mod_mlp[None, :, 0, :], mod_mlp[None, :, 1, :])
    piece = lax.all_gather(mlp_mod, "tensor", axis=0, tiled=True)
    grown = jnp.dot(piece.reshape(-1, model_width), mlp_expand, preferred_element_type=jnp.float32)
    activated = jax.nn.gelu(grown, approximate=True).astype(jnp.bfloat16)
    text_out = (text_own.astype(jnp.float32) + mod_text[None, :, 2, :] * text_sum).astype(
        jnp.bfloat16
    )
    mlp_term = jnp.dot(activated, mlp_reduce, preferred_element_type=jnp.float32).reshape(
        image_count, requests, model_width
    )
    mlp_sum = sum_over_tensor(mlp_term, owners, NARROW_SUMS)
    image_out = (image_mid.astype(jnp.float32) + mod_mlp[None, :, 2, :] * mlp_sum).astype(
        jnp.bfloat16
    )
    final_in = modulate(image_out, mod_final[None, :, 0, :], mod_final[None, :, 1, :])
    velocity = jnp.dot(
        final_in.reshape(own_image * requests, model_width),
        final_weight,
        preferred_element_type=jnp.float32,
    ).reshape(own_image, requests, final_weight.shape[1])
    velocity = velocity.transpose(1, 0, 2).reshape(
        requests, tile_rows, tile_cols * final_weight.shape[1]
    )
    step_float = step_index.astype(jnp.float32)
    time_delta = sigma_of(step_float + 1.0) - sigma_of(step_float)
    latents_next = latents + time_delta[:, None, None] * velocity
    latents_ext = padded(latents_next, (("tile", 1),), 1)
    image_out = image_out.transpose(1, 0, 2).reshape(requests, tile_rows, tile_cols, model_width)
    return (image_out, text_out.transpose(1, 0, 2), latents_ext)


def solution(mesh):
    return jax.shard_map(
        per_device,
        mesh=mesh,
        in_specs=(
            P(None, "tile", "tensor", None),
            P(None, ("tile", "tensor"), None),
            P(None, "tile", "tensor"),
            P(),
            P(),
            P(),
            P(),
            P(),
            P(),
            P(),
            P(None, None, "tensor"),
            P(None, None, "tensor"),
            P("tensor", None),
            P("tensor", None),
            P(),
            P(None, "tensor"),
            P("tensor", None),
            P(),
        ),
        out_specs=(
            P(None, "tile", "tensor", None),
            P(None, ("tile", "tensor"), None),
            P(None, "tile", "tensor"),
        ),
        check_vma=False,
    )
```

profile of v0, /device:TPU:97, one launch (start us, length us, event | category | flops | bytes accessed | tf_op | source)
XLA Modules:
  0.0 343.5 jit_solution(16405498130412113823)
XLA Ops:
  7.2 1.1 copy.54
  8.7 1.0 slice_bitcast_fusion.9
  9.7 0.8 add_convert_fusion.1
  10.6 1.0 fusion.66
  11.8 0.7 slice_bitcast_fusion.4
  12.6 1.3 broadcast_in_dim.42
  13.9 6.8 %all-to-all-start = ((bf16[16,2,8,3072]{3,2,1,0:T(8,128)(2,1)}), bf16[16,2,8,3072]{3,2,1,0:T(8,128)(2,1)}, u32[]{:S(2)}, u32[]{:S(2)}) async-start(bf16[16,2,8,3072]{3,2,1,0:T(8,128)(2,1)} %broadcast_in_dim.42), calls=%async_computation | async-start | bytes 3145728 | tf_op jit(solution)/shard_map/all_to_all | solution.py:126
  20.7 4.3 %copy.57 = bf16[3072,3,128]{0,2,1:T(8,128)(2,1)} copy(bf16[3072,3,128]{2,0,1:T(8,128)(2,1)} %param.28) | data formatting | bytes 4718592 | tf_op args[10]
  25.3 4.3 %copy.56 = bf16[3072,3,128]{0,2,1:T(8,128)(2,1)} copy(bf16[3072,3,128]{2,0,1:T(8,128)(2,1)} %param.29) | data formatting | bytes 4718592 | tf_op args[11]
  29.6 0.6 and_select_fusion.2
  30.2 0.5 compare_and_fusion
  30.8 0.6 compare_select_fusion
  31.3 0.6 iota_and_fusion
  31.9 14.3 %all-to-all-done = bf16[16,2,8,3072]{3,2,1,0:T(8,128)(2,1)} async-done(((bf16[16,2,8,3072]{3,2,1,0:T(8,128)(2,1)}), bf16[16,2,8,3072]{3,2,1,0:T(8,128)(2,1)}, u32[]{:S(2)}, u32[]{:S(2)}) %all-to-all-start) | async-done | bytes 1572896 | tf_op jit(solution)/shard_map/all_to_all | solution.py:126
  46.2 3.1 fusion.13
  49.8 0.7 copy.65
  50.5 0.7 copy.62
  51.3 24.4 %all-gather.3.cloned.1.call-done = bf16[64,8,3072]{2,1,0:T(8,128)(2,1)} async-done(((bf16[4,8,3072]{2,1,0:T(8,128)(2,1)}), bf16[64,8,3072]{2,1,0:T(8,128)(2,1)}) %all-gather.3.cloned.1.call-update) | async-done | bytes 3145744 | tf_op jit(solution)/shard_map/all_gather | solution.py:123
  75.7 4.0 %fusion.3 = f32[512,3,128]{0,2,1:T(8,128)S(1)} fusion(bf16[64,8,3072]{2,1,0:T(8,128)(2,1)} %all-gather.3.cloned.1.call-done, bf16[3072,3,128]{0,2,1:T(8,128)(2,1)} %copy.57), kind=kOutput, calls=%fused_computation.10 | convolution fusion | flops 1207959552 | bytes 6291456 | tf_op jit(solution)/shard_map/dot_general | solution.py:146
  80.2 0.7 fusion.83
  80.9 2.1 fusion.60
  83.2 0.9 pad_maximum_fusion.3
  84.3 0.7 copy.67
  85.0 0.9 pad_maximum_fusion.2
  86.3 2.0 pad_maximum_fusion
  88.3 7.9 %all-to-all-start.1 = ((bf16[16,240,1,128]{3,1,2,0:T(8,128)(2,1)}), bf16[16,240,1,128]{3,1,2,0:T(8,128)(2,1)}, u32[]{:S(2)}, u32[]{:S(2)}) async-start(bf16[16,240,1,128]{3,1,2,0:T(8,128)(2,1)} %pad_maximum_fusion), calls=%async_computation.1 | async-start | bytes 1966080 | tf_op jit(solution)/shard_map/all_to_all | solution.py:186
  96.2 0.6 dynamic_slice.3
  96.8 0.7 fusion.95
  97.5 23.7 %all-to-all-done.1 = bf16[16,240,1,128]{3,1,2,0:T(8,128)(2,1)} async-done(((bf16[16,240,1,128]{3,1,2,0:T(8,128)(2,1)}), bf16[16,240,1,128]{3,1,2,0:T(8,128)(2,1)}, u32[]{:S(2)}, u32[]{:S(2)}) %all-to-all-start.1) | async-done | bytes 983072 | tf_op jit(solution)/shard_map/all_to_all | solution.py:186
  121.1 1.2 fusion.105
  122.3 0.9 slice.176
  123.2 0.9 select_reduce_fusion
  124.1 1.1 fusion.1
  125.2 0.9 fusion.19
  126.1 13.0 %all_to_all.30 = bf16[16,48,128]{2,1,0:T(8,128)(2,1)S(1)} all-to-all(bf16[16,48,128]{2,1,0:T(8,128)(2,1)S(1)} %bitcast.211), channel_id=1, replica_groups=mesh['tile'=16,'tensor'=16] {'tile'}, dimensions={0} | all-to-all | bytes 393216 | tf_op jit(solution)/shard_map/all_to_all | solution.py:215
  139.1 0.7 copy-done.3
  139.8 2.6 convolution_convert_fusion
  142.5 4.6 %all-to-all-start.3 = ((bf16[16,4,8,3072]{3,2,1,0:T(8,128)(2,1)}), bf16[16,4,8,3072]{3,2,1,0:T(8,128)(2,1)}, u32[]{:S(2)}, u32[]{:S(2)}) async-start(bf16[16,4,8,3072]{3,2,1,0:T(8,128)(2,1)} %bitcast.191), calls=%async_computation.3 | async-start | bytes 6291456 | tf_op jit(solution)/shard_map/all_to_all | solution.py:82
  147.1 0.2 all-gather.5.cloned.1.call-start
  147.3 0.7 slice_bitcast_fusion.6
  148.0 46.9 %all-to-all-done.3 = bf16[16,4,8,3072]{3,2,1,0:T(8,128)(2,1)} async-done(((bf16[16,4,8,3072]{3,2,1,0:T(8,128)(2,1)}), bf16[16,4,8,3072]{3,2,1,0:T(8,128)(2,1)}, u32[]{:S(2)}, u32[]{:S(2)}) %all-to-all-start.3) | async-done | bytes 3145760 | tf_op jit(solution)/shard_map/all_to_all | solution.py:82
  194.9 2.5 convert_reduce_fusion.1
  197.6 0.2 fusion.42
  197.9 0.8 fusion.45
  198.7 0.5 slice.179
  199.9 3.0 fusion
  202.9 4.4 %all-to-all-start.5 = ((bf16[16,2,8,3072]{3,2,1,0:T(8,128)(2,1)}), bf16[16,2,8,3072]{3,2,1,0:T(8,128)(2,1)}, u32[]{:S(2)}, u32[]{:S(2)}) async-start(bf16[16,2,8,3072]{3,2,1,0:T(8,128)(2,1)} %bitcast.192), calls=%async_computation.5 | async-start | bytes 3145728 | tf_op jit(solution)/shard_map/all_to_all | solution.py:82
  207.3 52.4 %all-gather.5.cloned.1.call-done = bf16[64,8,3072]{2,1,0:T(8,128)(2,1)} async-done(((bf16[4,8,3072]{2,1,0:T(8,128)(2,1)}), bf16[64,8,3072]{2,1,0:T(8,128)(2,1)}) %all-gather.5.cloned.1.call-update) | async-done | bytes 3145744 | tf_op jit(solution)/shard_map/all_gather | solution.py:232
  259.7 7.8 %convolution_convert_fusion.1 = bf16[512,3072]{1,0:T(8,128)(2,1)} fusion(bf16[384,3072]{1,0:T(8,128)(2,1)S(1)} %copy-done, bf16[3072,384]{1,0:T(8,128)(2,1)} %param.33, bf16[64,8,3072]{2,1,0:T(8,128)(2,1)} %all-gather.5.cloned.1.call-done), kind=kOutput, calls=%fused_computation.5 | convolution fusion | flops 2419261440 | bytes 11010048 | tf_op jit(solution)/shard_map/dot_general | solution.py:238
  267.5 4.6 %all-to-all-start.4 = ((bf16[16,4,8,3072]{3,2,1,0:T(8,128)(2,1)}), bf16[16,4,8,3072]{3,2,1,0:T(8,128)(2,1)}, u32[]{:S(2)}, u32[]{:S(2)}) async-start(bf16[16,4,8,3072]{3,2,1,0:T(8,128)(2,1)} %bitcast.193), calls=%async_computation.4 | async-start | bytes 6291456 | tf_op jit(solution)/shard_map/all_to_all | solution.py:82
  272.2 1.2 fusion.110
  273.4 0.7 copy_bitcast_fusion
  274.1 1.6 convert_reduce_fusion.2
  275.8 0.7 copy.74
  276.6 41.8 %all-to-all-done.4 = bf16[16,4,8,3072]{3,2,1,0:T(8,128)(2,1)} async-done(((bf16[16,4,8,3072]{3,2,1,0:T(8,128)(2,1)}), bf16[16,4,8,3072]{3,2,1,0:T(8,128)(2,1)}, u32[]{:S(2)}, u32[]{:S(2)}) %all-to-all-start.4) | async-done | bytes 3145760 | tf_op jit(solution)/shard_map/all_to_all | solution.py:82
  318.4 2.5 convert_reduce_fusion
  320.9 1.0 convert_reduce_fusion.4
  322.2 1.3 convolution_bitcast_fusion
  323.7 6.2 %collective-permute-start = (f32[8,1,128]{2,1,0:T(1,128)S(1)}, f32[8,1,128]{2,1,0:T(1,128)S(1)}, u32[]{:S(2)}, u32[]{:S(2)}) collective-permute-start(f32[8,1,128]{2,1,0:T(1,128)S(1)} %get-tuple-element.33), channel_id=1, source_target_pairs={{0,16},{16,32},{32,48},{48,64},{64,80},{80,96},{96,112},{112,128},... | collective-permute-start | bytes 12296 | tf_op jit(solution)/shard_map/ppermute | solution.py:21
  329.9 1.9 collective-permute-start.1
  331.9 1.1 fusion.52
  332.9 0.9 copy.73
  333.8 2.2 collective-permute-done.1
  336.1 0.6 pad_maximum_fusion.4
  (100 shorter events, 3.1 us)
Async XLA Ops:
  7.2 252.6 %copy-start = (bf16[384,3072]{1,0:T(8,128)(2,1)S(1)}, bf16[384,3072]{1,0:T(8,128)(2,1)}, u32[]{:S(2)}) copy-start(bf16[384,3072]{1,0:T(8,128)(2,1)} %param.34) | copy-start | bytes 7077892
  7.2 4.4 %copy-start.2 = (bf16[8,2,3072]{2,1,0:T(2,128)(2,1)S(1)}, bf16[8,2,3072]{2,1,0:T(2,128)(2,1)}, u32[]{:S(2)}) copy-start(bf16[8,2,3072]{2,1,0:T(2,128)(2,1)} %param.19) | copy-start | bytes 294916
  7.2 4.6 %copy-start.10 = (f32[8,3,3072]{2,0,1:T(8,128)S(1)}, f32[8,3,3072]{2,0,1:T(8,128)}, u32[]{:S(2)}) copy-start(f32[8,3,3072]{2,0,1:T(8,128)} %param.25) | copy-start | bytes 884740
  7.2 68.5 %all-gather.3.cloned.1.call-start = ((), (), s32[]{:S(2)}) async-start(), calls=%async_computation.6 | async-start | bytes 3342336 | tf_op jit(solution)/shard_map/all_gather | solution.py:123
  13.9 32.3 %all-to-all-start = ((bf16[16,2,8,3072]{3,2,1,0:T(8,128)(2,1)}), bf16[16,2,8,3072]{3,2,1,0:T(8,128)(2,1)}, u32[]{:S(2)}, u32[]{:S(2)}) async-start(bf16[16,2,8,3072]{3,2,1,0:T(8,128)(2,1)} %broadcast_in_dim.42), calls=%async_computation | async-start | bytes 3145728 | tf_op jit(solution)/shard_map/all_to_all | solution.py:126
  20.7 4.3 %copy-start.14 = (s32[8,2]{0,1:T(2,128)S(1)}, s32[8,2]{0,1:T(2,128)}, u32[]{:S(2)}) copy-start(s32[8,2]{0,1:T(2,128)} %param.22) | copy-start | bytes 196
  25.0 6.9 %copy-start.13 = (f32[2,2,128]{2,1,0:T(2,128)S(1)}, f32[2,2,128]{2,1,0:T(2,128)}, u32[]{:S(2)}) copy-start(f32[2,2,128]{2,1,0:T(2,128)} %param.32) | copy-start | bytes 6148
  79.7 1.1 copy-start.15
  79.8 1.1 copy-start.16
  79.8 1.1 copy-start.17
  79.8 1.1 copy-start.18
  79.8 1.0 copy-start.19
  79.8 1.0 copy-start.20
  85.0 11.2 %copy-start.21 = (s32[8]{0:T(128)S(1)}, s32[8]{0:T(128)}, u32[]{:S(2)}) copy-start(s32[8]{0:T(128)} %param.23) | copy-start | bytes 100
  88.3 32.8 %all-to-all-start.1 = ((bf16[16,240,1,128]{3,1,2,0:T(8,128)(2,1)}), bf16[16,240,1,128]{3,1,2,0:T(8,128)(2,1)}, u32[]{:S(2)}, u32[]{:S(2)}) async-start(bf16[16,240,1,128]{3,1,2,0:T(8,128)(2,1)} %pad_maximum_fusion), calls=%async_computation.1 | async-start | bytes 1966080 | tf_op jit(solution)/shard_map/all_to_all | solution.py:186
  125.2 14.6 %copy-start.4 = (bf16[128,3072]{1,0:T(8,128)(2,1)S(1)}, bf16[128,3072]{1,0:T(8,128)(2,1)}, u32[]{:S(2)}) copy-start(bf16[128,3072]{1,0:T(8,128)(2,1)} %param.30) | copy-start | bytes 2359300
  139.1 0.7 copy-start.3
  142.5 4.9 %copy-start.11 = (f32[8,3,3072]{2,0,1:T(8,128)S(1)}, f32[8,3,3072]{2,0,1:T(8,128)}, u32[]{:S(2)}) copy-start(f32[8,3,3072]{2,0,1:T(8,128)} %param.26) | copy-start | bytes 884740
  142.5 52.5 %all-to-all-start.3 = ((bf16[16,4,8,3072]{3,2,1,0:T(8,128)(2,1)}), bf16[16,4,8,3072]{3,2,1,0:T(8,128)(2,1)}, u32[]{:S(2)}, u32[]{:S(2)}) async-start(bf16[16,4,8,3072]{3,2,1,0:T(8,128)(2,1)} %bitcast.191), calls=%async_computation.3 | async-start | bytes 6291456 | tf_op jit(solution)/shard_map/all_to_all | solution.py:82
  147.1 112.6 %all-gather.5.cloned.1.call-start = ((), (), s32[]{:S(2)}) async-start(), calls=%async_computation.7 | async-start | bytes 3342336 | tf_op jit(solution)/shard_map/all_gather | solution.py:232
  194.9 3.0 copy-start.5
  194.9 3.0 copy-start.6
  197.5 5.4 %copy-start.1 = (f32[4,8,3072]{2,1,0:T(8,128)}, f32[4,8,3072]{2,1,0:T(8,128)S(1)}, u32[]{:S(2)}) copy-start(f32[4,8,3072]{2,1,0:T(8,128)S(1)} %convert_reduce_fusion.1) | copy-start | bytes 1179652
  202.9 64.6 %all-to-all-start.5 = ((bf16[16,2,8,3072]{3,2,1,0:T(8,128)(2,1)}), bf16[16,2,8,3072]{3,2,1,0:T(8,128)(2,1)}, u32[]{:S(2)}, u32[]{:S(2)}) async-start(bf16[16,2,8,3072]{3,2,1,0:T(8,128)(2,1)} %bitcast.192), calls=%async_computation.5 | async-start | bytes 3145728 | tf_op jit(solution)/shard_map/all_to_all | solution.py:82
  267.5 4.7 %copy-start.22 = (s32[8]{0:T(128)S(1)}, s32[8]{0:T(128)}, u32[]{:S(2)}) copy-start(s32[8]{0:T(128)} %param.21) | copy-start | bytes 100
  267.5 8.2 %copy-start.9 = (f32[8,3072]{1,0:T(8,128)S(1)}, f32[8,3072]{1,0:T(8,128)}, u32[]{:S(2)}) copy-start(f32[8,3072]{1,0:T(8,128)} %get-tuple-element.14) | copy-start | bytes 294916
  267.5 50.9 %all-to-all-start.4 = ((bf16[16,4,8,3072]{3,2,1,0:T(8,128)(2,1)}), bf16[16,4,8,3072]{3,2,1,0:T(8,128)(2,1)}, u32[]{:S(2)}, u32[]{:S(2)}) async-start(bf16[16,4,8,3072]{3,2,1,0:T(8,128)(2,1)} %bitcast.193), calls=%async_computation.4 | async-start | bytes 6291456 | tf_op jit(solution)/shard_map/all_to_all | solution.py:82
  275.7 47.8 %copy-start.12 = (f32[8,2,128]{2,1,0:T(2,128)S(1)}, f32[8,2,128]{2,1,0:T(2,128)}, u32[]{:S(2)}) copy-start(f32[8,2,128]{2,1,0:T(2,128)} %param.20) | copy-start | bytes 24580
  275.8 46.4 %copy-start.7 = (f32[8,3072]{1,0:T(8,128)S(1)}, f32[8,3072]{1,0:T(8,128)}, u32[]{:S(2)}) copy-start(f32[8,3072]{1,0:T(8,128)} %get-tuple-element.55) | copy-start | bytes 294916
  318.4 3.8 %copy-start.8 = (f32[8,3072]{1,0:T(8,128)S(1)}, f32[8,3072]{1,0:T(8,128)}, u32[]{:S(2)}) copy-start(f32[8,3072]{1,0:T(8,128)} %get-tuple-element.56) | copy-start | bytes 294916
  323.7 10.1 %collective-permute-start = (f32[8,1,128]{2,1,0:T(1,128)S(1)}, f32[8,1,128]{2,1,0:T(1,128)S(1)}, u32[]{:S(2)}, u32[]{:S(2)}) collective-permute-start(f32[8,1,128]{2,1,0:T(1,128)S(1)} %get-tuple-element.33), channel_id=1, source_target_pairs={{0,16},{16,32},{32,48},{48,64},{64,80},{80,96},{96,112},{112,128},... | collective-permute-start | bytes 12296 | tf_op jit(solution)/shard_map/ppermute | solution.py:21
  329.9 6.1 %collective-permute-start.1 = (f32[8,1,128]{2,1,0:T(1,128)S(1)}, f32[8,1,128]{2,1,0:T(1,128)S(1)}, u32[]{:S(2)}, u32[]{:S(2)}) collective-permute-start(f32[8,1,128]{2,1,0:T(1,128)S(1)} %get-tuple-element.34), channel_id=1, source_target_pairs={{16,0},{32,16},{48,32},{64,48},{80,64},{96,80},{112,96},{128,112},... | collective-permute-start | bytes 12296 | tf_op jit(solution)/shard_map/ppermute | solution.py:22
Sparse Core Ops, SparseCore 0:
  11.0 64.6 all-gather.2
  198.8 60.8 all-gather.4
where the time goes:
time: 345 us; the launch traced here: 344 us
  waiting for transfers between devices  206 us (60%)
  starting transfers between devices  36.8 us (11%)
  other arithmetic  27.1 us (8%)
  matrix products  23.7 us (7%)
  local copies, waits for them, and re-layouts  21.9 us (6%)
  between operations  15.2 us (4%)
  blocking collectives  13 us (4%)
    all_to_all x3, waiting for transfers between devices, sum_over_tensor(): parts = lax.all_to_all(parts, 'tensor', 0, 0, tiled=True)  88.7 us
    all_gather x1, waiting for transfers between devices, per_device(): piece = lax.all_gather(mlp_mod, 'tensor', axis=0, tiled=True)  52.4 us
    all_gather x1, waiting for transfers between devices, per_device(): lax.all_gather(image_mod_own, 'tensor', axis=0, tiled=True)  24.4 us
    all_to_all x1, waiting for transfers between devices, per_device(): incoming = lax.all_to_all(outgoing, 'tile', 0, 0, tiled=True)  23.7 us
    all_to_all x1, waiting for transfers between devices, per_device(): lax.all_to_all(jnp.broadcast_to(text_mod_own[None], (owners,) + text_mod_...  14.3 us
    all_to_all x3, starting transfers between devices, sum_over_tensor(): parts = lax.all_to_all(parts, 'tensor', 0, 0, tiled=True)  13.6 us
    all_to_all x1, blocking collectives, per_device(): returned = lax.all_to_all(attended_mine, 'tile', 0, 0, tiled=True)  13 us
    unnamed x50, local copies, waits for them, and re-layouts  11 us
  transfers between devices with their start and end apart: 9, of which 7 were waited for; matrix products, arithmetic and copies ran while one was open for 11% of the time, Pallas kernels for 0%

commit v1 on v0

--- a/solution.py
+++ b/solution.py
@@ -9,6 +9,20 @@
 NSTEPS = 28
 norm_eps = 1e-06
 time_shift = 3.0
+
+
+def array_advance(my_data, which_dim, content):
+    met_up = my_data.shape
+    mat_out = my_data.reshape(
+        *met_up[:which_dim], content, met_up[which_dim] // content, *met_up[which_dim + 1 :]
+    )
+    return jnp.moveaxis(mat_out, which_dim, 0)
+
+
+def trace_the_paths(sample, dim_no):
+    block_last = list(sample.shape[1:])
+    block_last[dim_no] *= sample.shape[0]
+    return jnp.moveaxis(sample, 0, dim_no).reshape(block_last)
 
 
 def padded(value, sides, width):
@@ -183,7 +197,22 @@
     values_r = jnp.repeat(values.transpose(1, 0, 2, 3), parts, axis=0)
     query_r = query.transpose(1, 0, 2, 3).reshape(tiles, part_len, local_heads, HEAD_DIM)
     outgoing = jnp.concatenate([keys_r, values_r, query_r], 1)
-    incoming = lax.all_to_all(outgoing, "tile", 0, 0, tiled=True)
+
+    def part_windows_on_mesh(incoming_x, peer_axis, vec, obj):
+        current_block, found_now = (lax.axis_size(peer_axis), lax.axis_index(peer_axis))
+        m_next = array_advance(incoming_x, vec, current_block)
+        all_rows = [m_next[found_now]]
+        ii = 1
+        while ii < current_block:
+            g_now = m_next[found_now ^ ii]
+            all_rows.append(
+                lax.ppermute(g_now, peer_axis, [(ix, ix ^ ii) for ix in range(current_block)])
+            )
+            ii += 1
+        m_next = jnp.stack(all_rows, axis=0)[found_now ^ jnp.arange(current_block)]
+        return trace_the_paths(m_next, obj)
+
+    incoming = part_windows_on_mesh(outgoing, "tile", 0, 0)
     keys_all = incoming[:, :block_len].reshape(tiles * block_len, local_heads, HEAD_DIM)
     values_all = incoming[:, block_len : 2 * block_len].reshape(
         tiles * block_len, local_heads, HEAD_DIM

time: 345 us -> 354 us (1.026)
  waiting for transfers between devices: 206 us -> 185 us
  starting transfers between devices: 36.8 us -> 55 us
  local copies, waits for them, and re-layouts: 21.9 us -> 36.3 us
    ppermute x0 -> x15, starting transfers between devices: none -> 26.3 us  [part_windows_on_mesh(): lax.ppermute(g_now, peer_axis, [(ix, ix ^ ii) for ix in range(current_blo...]
    all_to_all x1 -> x0, waiting for transfers between devices: 23.7 us -> none  [per_device(): incoming = lax.all_to_all(outgoing, 'tile', 0, 0, tiled=True)]
    unnamed x50 -> x71, local copies, waits for them, and re-layouts: 11 us -> 20.4 us
    all_to_all x1 -> x0, starting transfers between devices: 7.93 us -> none  [per_device(): incoming = lax.all_to_all(outgoing, 'tile', 0, 0, tiled=True)]
    ppermute x0 -> x15, waiting for transfers between devices: none -> 4.29 us  [part_windows_on_mesh(): lax.ppermute(g_now, peer_axis, [(ix, ix ^ ii) for ix in range(current_blo...]
  transfers between devices with their start and end apart: 9 -> 23, of which waited for: 7 -> 8; matrix products, arithmetic and copies ran while one was open for 11% -> 14% of each run, Pallas kernels for 0% -> 0%
where the time goes in v1:
time: 354 us; the launch traced here: 353 us
  waiting for transfers between devices  185 us (52%)
  starting transfers between devices  55 us (16%)
  local copies, waits for them, and re-layouts  36.3 us (10%)
  other arithmetic  24.7 us (7%)
  matrix products  23.7 us (7%)
  between operations  15.4 us (4%)
  blocking collectives  13.2 us (4%)
    all_to_all x3, waiting for transfers between devices, sum_over_tensor(): parts = lax.all_to_all(parts, 'tensor', 0, 0, tiled=True)  88.9 us
    all_gather x1, waiting for transfers between devices, per_device(): piece = lax.all_gather(mlp_mod, 'tensor', axis=0, tiled=True)  52.5 us
    ppermute x15, starting transfers between devices, part_windows_on_mesh(): lax.ppermute(g_now, peer_axis, [(ix, ix ^ ii) for ix in range(current_blo...  26.3 us
    all_gather x1, waiting for transfers between devices, per_device(): lax.all_gather(image_mod_own, 'tensor', axis=0, tiled=True)  24.4 us
    unnamed x71, local copies, waits for them, and re-layouts  20.4 us
    all_to_all x3, starting transfers between devices, sum_over_tensor(): parts = lax.all_to_all(parts, 'tensor', 0, 0, tiled=True)  13.7 us
    all_to_all x1, blocking collectives, per_device(): returned = lax.all_to_all(attended_mine, 'tile', 0, 0, tiled=True)  13.2 us
    all_to_all x1, waiting for transfers between devices, per_device(): lax.all_to_all(jnp.broadcast_to(text_mod_own[None], (owners,) + text_mod_...  12.5 us
  transfers between devices with their start and end apart: 23, of which 8 were waited for; matrix products, arithmetic and copies ran while one was open for 14% of the time, Pallas kernels for 0%

profile of v1, /device:TPU:97, one launch (start us, length us, event | category | flops | bytes accessed | tf_op | source)
XLA Modules:
  0.0 353.0 jit_solution(3263528909424900870)
XLA Ops:
  7.2 1.1 copy.82
  8.7 1.0 slice_bitcast_fusion.9
  9.7 0.8 add_convert_fusion.1
  10.6 1.0 fusion.66
  12.6 1.3 broadcast_in_dim.42
  13.9 6.8 %all-to-all-start = ((bf16[16,2,8,3072]{3,2,1,0:T(8,128)(2,1)}), bf16[16,2,8,3072]{3,2,1,0:T(8,128)(2,1)}, u32[]{:S(2)}, u32[]{:S(2)}) async-start(bf16[16,2,8,3072]{3,2,1,0:T(8,128)(2,1)} %broadcast_in_dim.42), calls=%async_computation | async-start | bytes 3145728 | tf_op jit(solution)/shard_map/all_to_all | solution.py:140
  20.8 4.3 %copy.85 = bf16[3072,3,128]{0,2,1:T(8,128)(2,1)} copy(bf16[3072,3,128]{2,0,1:T(8,128)(2,1)} %param.28) | data formatting | bytes 4718592 | tf_op args[10]
  25.5 4.3 %copy.84 = bf16[3072,3,128]{0,2,1:T(8,128)(2,1)} copy(bf16[3072,3,128]{2,0,1:T(8,128)(2,1)} %param.29) | data formatting | bytes 4718592 | tf_op args[11]
  33.8 12.5 %all-to-all-done = bf16[16,2,8,3072]{3,2,1,0:T(8,128)(2,1)} async-done(((bf16[16,2,8,3072]{3,2,1,0:T(8,128)(2,1)}), bf16[16,2,8,3072]{3,2,1,0:T(8,128)(2,1)}, u32[]{:S(2)}, u32[]{:S(2)}) %all-to-all-start) | async-done | bytes 1572896 | tf_op jit(solution)/shard_map/all_to_all | solution.py:140
  46.2 3.1 fusion.13
  49.7 0.7 copy.87
  50.4 0.7 copy.93
  51.3 24.4 %all-gather.3.cloned.1.call-done = bf16[64,8,3072]{2,1,0:T(8,128)(2,1)} async-done(((bf16[4,8,3072]{2,1,0:T(8,128)(2,1)}), bf16[64,8,3072]{2,1,0:T(8,128)(2,1)}) %all-gather.3.cloned.1.call-update) | async-done | bytes 3145744 | tf_op jit(solution)/shard_map/all_gather | solution.py:137
  75.7 4.0 %fusion.3 = f32[512,3,128]{0,2,1:T(8,128)S(1)} fusion(bf16[64,8,3072]{2,1,0:T(8,128)(2,1)} %all-gather.3.cloned.1.call-done, bf16[3072,3,128]{0,2,1:T(8,128)(2,1)} %copy.85), kind=kOutput, calls=%fused_computation.11 | convolution fusion | flops 1207959552 | bytes 6291456 | tf_op jit(solution)/shard_map/dot_general | solution.py:160
  80.9 1.5 fusion.60
  82.6 0.7 copy.89
  83.3 0.9 pad_maximum_fusion.3
  84.4 0.9 pad_maximum_fusion.2
  85.5 1.0 broadcast_in_dim.77
  86.9 1.1 collective-permute-start
  88.2 1.5 collective-permute-start.2
  89.8 2.6 collective-permute-start.4
  93.7 3.5 collective-permute-start.6
  97.8 2.8 collective-permute-start.7
  101.2 2.9 collective-permute-start.8
  104.8 0.9 collective-permute-start.9
  106.3 3.8 %collective-permute-start.10 = (bf16[1,240,1,128]{3,1,2,0:T(8,128)(2,1)S(1)}, bf16[1,240,1,128]{3,1,2,0:T(8,128)(2,1)S(1)}, u32[]{:S(2)}, u32[]{:S(2)}) collective-permute-start(bf16[1,240,1,128]{3,1,2,0:T(8,128)(2,1)S(1)} %get-tuple-element.15), channel_id=1, source_target_pairs={{0,176},{16,160},{32,144},{48,128},{64,240},{80,224},{96,208},{112... | collective-permute-start | bytes 184328 | tf_op jit(solution)/shard_map/ppermute | solution.py:209
  110.8 1.7 collective-permute-start.11
  113.2 2.2 collective-permute-start.12
  116.0 2.5 collective-permute-start.13
  122.0 3.6 %collective-permute-done.13 = bf16[1,240,1,128]{3,1,2,0:T(8,128)(2,1)S(1)} collective-permute-done((bf16[1,240,1,128]{3,1,2,0:T(8,128)(2,1)S(1)}, bf16[1,240,1,128]{3,1,2,0:T(8,128)(2,1)S(1)}, u32[]{:S(2)}, u32[]{:S(2)}) %collective-permute-start.13) | collective-permute-done | bytes 61472 | tf_op jit(solution)/shard_map/ppermute | solution.py:209
  126.2 0.7 collective-permute-done.14
  127.5 2.8 gather_fusion
  130.3 1.2 fusion.107
  131.5 0.9 slice.178
  132.5 0.9 select_reduce_fusion
  133.3 1.1 fusion.1
  134.4 0.9 fusion.19
  135.4 13.2 %all_to_all.25 = bf16[16,48,128]{2,1,0:T(8,128)(2,1)S(1)} all-to-all(bf16[16,48,128]{2,1,0:T(8,128)(2,1)S(1)} %bitcast.262), channel_id=1, replica_groups=mesh['tile'=16,'tensor'=16] {'tile'}, dimensions={0} | all-to-all | bytes 393216 | tf_op jit(solution)/shard_map/all_to_all | solution.py:244
  148.5 0.7 copy-done.3
  149.2 2.7 convolution_convert_fusion
  151.9 4.6 %all-to-all-start.2 = ((bf16[16,4,8,3072]{3,2,1,0:T(8,128)(2,1)}), bf16[16,4,8,3072]{3,2,1,0:T(8,128)(2,1)}, u32[]{:S(2)}, u32[]{:S(2)}) async-start(bf16[16,4,8,3072]{3,2,1,0:T(8,128)(2,1)} %bitcast.240), calls=%async_computation.2 | async-start | bytes 6291456 | tf_op jit(solution)/shard_map/all_to_all | solution.py:96
  156.6 0.7 slice_bitcast_fusion.6
  157.3 47.0 %all-to-all-done.2 = bf16[16,4,8,3072]{3,2,1,0:T(8,128)(2,1)} async-done(((bf16[16,4,8,3072]{3,2,1,0:T(8,128)(2,1)}), bf16[16,4,8,3072]{3,2,1,0:T(8,128)(2,1)}, u32[]{:S(2)}, u32[]{:S(2)}) %all-to-all-start.2) | async-done | bytes 3145760 | tf_op jit(solution)/shard_map/all_to_all | solution.py:96
  204.3 2.5 convert_reduce_fusion.1
  207.3 0.8 fusion.45
  209.3 3.0 fusion
  212.3 4.4 %all-to-all-start.4 = ((bf16[16,2,8,3072]{3,2,1,0:T(8,128)(2,1)}), bf16[16,2,8,3072]{3,2,1,0:T(8,128)(2,1)}, u32[]{:S(2)}, u32[]{:S(2)}) async-start(bf16[16,2,8,3072]{3,2,1,0:T(8,128)(2,1)} %bitcast.241), calls=%async_computation.4 | async-start | bytes 3145728 | tf_op jit(solution)/shard_map/all_to_all | solution.py:96
  216.7 52.5 %all-gather.5.cloned.1.call-done = bf16[64,8,3072]{2,1,0:T(8,128)(2,1)} async-done(((bf16[4,8,3072]{2,1,0:T(8,128)(2,1)}), bf16[64,8,3072]{2,1,0:T(8,128)(2,1)}) %all-gather.5.cloned.1.call-update) | async-done | bytes 3145744 | tf_op jit(solution)/shard_map/all_gather | solution.py:261
  269.1 7.8 %convolution_convert_fusion.1 = bf16[512,3072]{1,0:T(8,128)(2,1)} fusion(bf16[384,3072]{1,0:T(8,128)(2,1)S(1)} %copy-done, bf16[3072,384]{1,0:T(8,128)(2,1)} %param.33, bf16[64,8,3072]{2,1,0:T(8,128)(2,1)} %all-gather.5.cloned.1.call-done), kind=kOutput, calls=%fused_computation.6 | convolution fusion | flops 2419261440 | bytes 11010048 | tf_op jit(solution)/shard_map/dot_general | solution.py:267
  276.9 4.6 %all-to-all-start.3 = ((bf16[16,4,8,3072]{3,2,1,0:T(8,128)(2,1)}), bf16[16,4,8,3072]{3,2,1,0:T(8,128)(2,1)}, u32[]{:S(2)}, u32[]{:S(2)}) async-start(bf16[16,4,8,3072]{3,2,1,0:T(8,128)(2,1)} %bitcast.244), calls=%async_computation.3 | async-start | bytes 6291456 | tf_op jit(solution)/shard_map/all_to_all | solution.py:96
  281.6 1.2 fusion.112
  282.8 0.7 copy_bitcast_fusion
  283.5 1.6 convert_reduce_fusion.2
  285.3 0.7 copy.115
  286.0 41.8 %all-to-all-done.3 = bf16[16,4,8,3072]{3,2,1,0:T(8,128)(2,1)} async-done(((bf16[16,4,8,3072]{3,2,1,0:T(8,128)(2,1)}), bf16[16,4,8,3072]{3,2,1,0:T(8,128)(2,1)}, u32[]{:S(2)}, u32[]{:S(2)}) %all-to-all-start.3) | async-done | bytes 3145760 | tf_op jit(solution)/shard_map/all_to_all | solution.py:96
  327.8 2.5 convert_reduce_fusion
  330.4 1.0 convert_reduce_fusion.4
  331.6 1.3 convolution_bitcast_fusion
  333.1 6.2 %collective-permute-start.15 = (f32[8,1,128]{2,1,0:T(1,128)S(1)}, f32[8,1,128]{2,1,0:T(1,128)S(1)}, u32[]{:S(2)}, u32[]{:S(2)}) collective-permute-start(f32[8,1,128]{2,1,0:T(1,128)S(1)} %get-tuple-element.49), channel_id=1, source_target_pairs={{0,16},{16,32},{32,48},{48,64},{64,80},{80,96},{96,112},{112,128},... | collective-permute-start | bytes 12296 | tf_op jit(solution)/shard_map/ppermute | solution.py:35
  339.4 1.9 collective-permute-start.16
  341.3 1.1 fusion.52
  342.4 0.9 copy.114
  343.3 2.2 collective-permute-done.16
  (155 shorter events, 21.0 us)
Async XLA Ops:
  7.2 262.0 %copy-start = (bf16[384,3072]{1,0:T(8,128)(2,1)S(1)}, bf16[384,3072]{1,0:T(8,128)(2,1)}, u32[]{:S(2)}) copy-start(bf16[384,3072]{1,0:T(8,128)(2,1)} %param.34) | copy-start | bytes 7077892
  7.2 4.4 %copy-start.2 = (bf16[8,2,3072]{2,1,0:T(2,128)(2,1)S(1)}, bf16[8,2,3072]{2,1,0:T(2,128)(2,1)}, u32[]{:S(2)}) copy-start(bf16[8,2,3072]{2,1,0:T(2,128)(2,1)} %param.19) | copy-start | bytes 294916
  7.2 4.6 %copy-start.10 = (f32[8,3,3072]{2,0,1:T(8,128)S(1)}, f32[8,3,3072]{2,0,1:T(8,128)}, u32[]{:S(2)}) copy-start(f32[8,3,3072]{2,0,1:T(8,128)} %param.25) | copy-start | bytes 884740
  7.2 68.5 %all-gather.3.cloned.1.call-start = ((), (), s32[]{:S(2)}) async-start(), calls=%async_computation.5 | async-start | bytes 3342336 | tf_op jit(solution)/shard_map/all_gather | solution.py:137
  10.6 10.2 %copy-start.17 = (s32[8,2]{0,1:T(2,128)S(1)}, s32[8,2]{0,1:T(2,128)}, u32[]{:S(2)}) copy-start(s32[8,2]{0,1:T(2,128)} %param.22) | copy-start | bytes 196
  13.9 32.3 %all-to-all-start = ((bf16[16,2,8,3072]{3,2,1,0:T(8,128)(2,1)}), bf16[16,2,8,3072]{3,2,1,0:T(8,128)(2,1)}, u32[]{:S(2)}, u32[]{:S(2)}) async-start(bf16[16,2,8,3072]{3,2,1,0:T(8,128)(2,1)} %broadcast_in_dim.42), calls=%async_computation | async-start | bytes 3145728 | tf_op jit(solution)/shard_map/all_to_all | solution.py:140
  25.1 4.7 %copy-start.24 = (s32[8]{0:T(128)S(1)}, s32[8]{0:T(128)}, u32[]{:S(2)}) copy-start(s32[8]{0:T(128)} %param.23) | copy-start | bytes 100
  25.1 8.1 %copy-start.16 = (f32[2,2,128]{2,1,0:T(2,128)S(1)}, f32[2,2,128]{2,1,0:T(2,128)}, u32[]{:S(2)}) copy-start(f32[2,2,128]{2,1,0:T(2,128)} %param.32) | copy-start | bytes 6148
  51.3 28.6 %copy-start.14 = (f32[128]{0:T(128)S(1)}, f32[128]{0:T(128)}, u32[]{:S(2)}) copy-start(f32[128]{0:T(128)} %get-tuple-element.54) | copy-start | bytes 1540
  51.3 28.6 %copy-start.15 = (f32[128]{0:T(128)S(1)}, f32[128]{0:T(128)}, u32[]{:S(2)}) copy-start(f32[128]{0:T(128)} %get-tuple-element.55) | copy-start | bytes 1540
  79.7 1.1 copy-start.18
  79.8 1.1 copy-start.19
  79.8 1.1 copy-start.20
  79.8 1.1 copy-start.21
  79.8 1.1 copy-start.22
  79.8 1.1 copy-start.23
  79.8 2.6 copy-start.12
  86.9 6.1 %collective-permute-start = (bf16[1,240,1,128]{3,1,2,0:T(8,128)(2,1)S(1)}, bf16[1,240,1,128]{3,1,2,0:T(8,128)(2,1)S(1)}, u32[]{:S(2)}, u32[]{:S(2)}) collective-permute-start(bf16[1,240,1,128]{3,1,2,0:T(8,128)(2,1)S(1)} %get-tuple-element.25), channel_id=1, source_target_pairs={{0,16},{16,0},{32,48},{48,32},{64,80},{80,64},{96,112},{112,96},{1... | collective-permute-start | bytes 184328 | tf_op jit(solution)/shard_map/ppermute | solution.py:209
  88.0 5.8 %collective-permute-start.1 = (bf16[1,240,1,128]{3,1,2,0:T(8,128)(2,1)S(1)}, bf16[1,240,1,128]{3,1,2,0:T(8,128)(2,1)S(1)}, u32[]{:S(2)}, u32[]{:S(2)}) collective-permute-start(bf16[1,240,1,128]{3,1,2,0:T(8,128)(2,1)S(1)} %get-tuple-element.24), channel_id=1, source_target_pairs={{0,32},{16,48},{32,0},{48,16},{64,96},{80,112},{96,64},{112,80},{1... | collective-permute-start | bytes 184328 | tf_op jit(solution)/shard_map/ppermute | solution.py:209
  88.2 9.7 %collective-permute-start.2 = (bf16[1,240,1,128]{3,1,2,0:T(8,128)(2,1)S(1)}, bf16[1,240,1,128]{3,1,2,0:T(8,128)(2,1)S(1)}, u32[]{:S(2)}, u32[]{:S(2)}) collective-permute-start(bf16[1,240,1,128]{3,1,2,0:T(8,128)(2,1)S(1)} %get-tuple-element.23), channel_id=1, source_target_pairs={{0,48},{16,32},{32,16},{48,0},{64,112},{80,96},{96,80},{112,64},{1... | collective-permute-start | bytes 184328 | tf_op jit(solution)/shard_map/ppermute | solution.py:209
  89.7 11.6 %collective-permute-start.3 = (bf16[1,240,1,128]{3,1,2,0:T(8,128)(2,1)S(1)}, bf16[1,240,1,128]{3,1,2,0:T(8,128)(2,1)S(1)}, u32[]{:S(2)}, u32[]{:S(2)}) collective-permute-start(bf16[1,240,1,128]{3,1,2,0:T(8,128)(2,1)S(1)} %get-tuple-element.22), channel_id=1, source_target_pairs={{0,64},{16,80},{32,96},{48,112},{64,0},{80,16},{96,32},{112,48},{1... | collective-permute-start | bytes 184328 | tf_op jit(solution)/shard_map/ppermute | solution.py:209
  89.8 15.0 %collective-permute-start.4 = (bf16[1,240,1,128]{3,1,2,0:T(8,128)(2,1)S(1)}, bf16[1,240,1,128]{3,1,2,0:T(8,128)(2,1)S(1)}, u32[]{:S(2)}, u32[]{:S(2)}) collective-permute-start(bf16[1,240,1,128]{3,1,2,0:T(8,128)(2,1)S(1)} %get-tuple-element.21), channel_id=1, source_target_pairs={{0,80},{16,64},{32,112},{48,96},{64,16},{80,0},{96,48},{112,32},{1... | collective-permute-start | bytes 184328 | tf_op jit(solution)/shard_map/ppermute | solution.py:209
  93.0 13.3 %collective-permute-start.5 = (bf16[1,240,1,128]{3,1,2,0:T(8,128)(2,1)S(1)}, bf16[1,240,1,128]{3,1,2,0:T(8,128)(2,1)S(1)}, u32[]{:S(2)}, u32[]{:S(2)}) collective-permute-start(bf16[1,240,1,128]{3,1,2,0:T(8,128)(2,1)S(1)} %get-tuple-element.20), channel_id=1, source_target_pairs={{0,96},{16,112},{32,64},{48,80},{64,32},{80,48},{96,0},{112,16},{1... | collective-permute-start | bytes 184328 | tf_op jit(solution)/shard_map/ppermute | solution.py:209
  93.7 17.0 %collective-permute-start.6 = (bf16[1,240,1,128]{3,1,2,0:T(8,128)(2,1)S(1)}, bf16[1,240,1,128]{3,1,2,0:T(8,128)(2,1)S(1)}, u32[]{:S(2)}, u32[]{:S(2)}) collective-permute-start(bf16[1,240,1,128]{3,1,2,0:T(8,128)(2,1)S(1)} %get-tuple-element.19), channel_id=1, source_target_pairs={{0,112},{16,96},{32,80},{48,64},{64,48},{80,32},{96,16},{112,0},{1... | collective-permute-start | bytes 184328 | tf_op jit(solution)/shard_map/ppermute | solution.py:209
  97.8 15.3 %collective-permute-start.7 = (bf16[1,240,1,128]{3,1,2,0:T(8,128)(2,1)S(1)}, bf16[1,240,1,128]{3,1,2,0:T(8,128)(2,1)S(1)}, u32[]{:S(2)}, u32[]{:S(2)}) collective-permute-start(bf16[1,240,1,128]{3,1,2,0:T(8,128)(2,1)S(1)} %get-tuple-element.18), channel_id=1, source_target_pairs={{0,128},{16,144},{32,160},{48,176},{64,192},{80,208},{96,224},{112... | collective-permute-start | bytes 184328 | tf_op jit(solution)/shard_map/ppermute | solution.py:209
  101.2 14.7 %collective-permute-start.8 = (bf16[1,240,1,128]{3,1,2,0:T(8,128)(2,1)S(1)}, bf16[1,240,1,128]{3,1,2,0:T(8,128)(2,1)S(1)}, u32[]{:S(2)}, u32[]{:S(2)}) collective-permute-start(bf16[1,240,1,128]{3,1,2,0:T(8,128)(2,1)S(1)} %get-tuple-element.17), channel_id=1, source_target_pairs={{0,144},{16,128},{32,176},{48,160},{64,208},{80,192},{96,240},{112... | collective-permute-start | bytes 184328 | tf_op jit(solution)/shard_map/ppermute | solution.py:209
  104.8 14.3 %collective-permute-start.9 = (bf16[1,240,1,128]{3,1,2,0:T(8,128)(2,1)S(1)}, bf16[1,240,1,128]{3,1,2,0:T(8,128)(2,1)S(1)}, u32[]{:S(2)}, u32[]{:S(2)}) collective-permute-start(bf16[1,240,1,128]{3,1,2,0:T(8,128)(2,1)S(1)} %get-tuple-element.16), channel_id=1, source_target_pairs={{0,160},{16,176},{32,128},{48,144},{64,224},{80,240},{96,192},{112... | collective-permute-start | bytes 184328 | tf_op jit(solution)/shard_map/ppermute | solution.py:209
  106.3 13.8 %collective-permute-start.10 = (bf16[1,240,1,128]{3,1,2,0:T(8,128)(2,1)S(1)}, bf16[1,240,1,128]{3,1,2,0:T(8,128)(2,1)S(1)}, u32[]{:S(2)}, u32[]{:S(2)}) collective-permute-start(bf16[1,240,1,128]{3,1,2,0:T(8,128)(2,1)S(1)} %get-tuple-element.15), channel_id=1, source_target_pairs={{0,176},{16,160},{32,144},{48,128},{64,240},{80,224},{96,208},{112... | collective-permute-start | bytes 184328 | tf_op jit(solution)/shard_map/ppermute | solution.py:209
  110.8 10.0 %collective-permute-start.11 = (bf16[1,240,1,128]{3,1,2,0:T(8,128)(2,1)S(1)}, bf16[1,240,1,128]{3,1,2,0:T(8,128)(2,1)S(1)}, u32[]{:S(2)}, u32[]{:S(2)}) collective-permute-start(bf16[1,240,1,128]{3,1,2,0:T(8,128)(2,1)S(1)} %get-tuple-element.14), channel_id=1, source_target_pairs={{0,192},{16,208},{32,224},{48,240},{64,128},{80,144},{96,160},{112... | collective-permute-start | bytes 184328 | tf_op jit(solution)/shard_map/ppermute | solution.py:209
  113.2 8.2 %collective-permute-start.12 = (bf16[1,240,1,128]{3,1,2,0:T(8,128)(2,1)S(1)}, bf16[1,240,1,128]{3,1,2,0:T(8,128)(2,1)S(1)}, u32[]{:S(2)}, u32[]{:S(2)}) collective-permute-start(bf16[1,240,1,128]{3,1,2,0:T(8,128)(2,1)S(1)} %get-tuple-element.13), channel_id=1, source_target_pairs={{0,208},{16,192},{32,240},{48,224},{64,144},{80,128},{96,176},{112... | collective-permute-start | bytes 184328 | tf_op jit(solution)/shard_map/ppermute | solution.py:209
  116.0 9.6 %collective-permute-start.13 = (bf16[1,240,1,128]{3,1,2,0:T(8,128)(2,1)S(1)}, bf16[1,240,1,128]{3,1,2,0:T(8,128)(2,1)S(1)}, u32[]{:S(2)}, u32[]{:S(2)}) collective-permute-start(bf16[1,240,1,128]{3,1,2,0:T(8,128)(2,1)S(1)} %get-tuple-element.12), channel_id=1, source_target_pairs={{0,224},{16,240},{32,192},{48,208},{64,160},{80,176},{96,128},{112... | collective-permute-start | bytes 184328 | tf_op jit(solution)/shard_map/ppermute | solution.py:209
  119.1 7.8 %collective-permute-start.14 = (bf16[1,240,1,128]{3,1,0,2:T(8,128)(2,1)S(1)}, bf16[1,240,1,128]{3,1,0,2:T(8,128)(2,1)S(1)}, u32[]{:S(2)}, u32[]{:S(2)}) collective-permute-start(bf16[1,240,1,128]{3,1,0,2:T(8,128)(2,1)S(1)} %constant_dynamic-slice_fusion), channel_id=1, source_target_pairs={{0,240},{16,224},{32,208},{48,192},{64,176},{80,160},{96,144},{112... | collective-permute-start | bytes 184328 | tf_op jit(solution)/shard_map/ppermute | solution.py:209
  134.4 14.8 %copy-start.4 = (bf16[128,3072]{1,0:T(8,128)(2,1)S(1)}, bf16[128,3072]{1,0:T(8,128)(2,1)}, u32[]{:S(2)}) copy-start(bf16[128,3072]{1,0:T(8,128)(2,1)} %param.30) | copy-start | bytes 2359300
  148.5 0.7 copy-start.3
  151.9 4.7 %copy-start.11 = (f32[8,3,3072]{2,0,1:T(8,128)S(1)}, f32[8,3,3072]{2,0,1:T(8,128)}, u32[]{:S(2)}) copy-start(f32[8,3,3072]{2,0,1:T(8,128)} %param.26) | copy-start | bytes 884740
  151.9 52.4 %all-to-all-start.2 = ((bf16[16,4,8,3072]{3,2,1,0:T(8,128)(2,1)}), bf16[16,4,8,3072]{3,2,1,0:T(8,128)(2,1)}, u32[]{:S(2)}, u32[]{:S(2)}) async-start(bf16[16,4,8,3072]{3,2,1,0:T(8,128)(2,1)} %bitcast.240), calls=%async_computation.2 | async-start | bytes 6291456 | tf_op jit(solution)/shard_map/all_to_all | solution.py:96
  156.5 112.6 %all-gather.5.cloned.1.call-start = ((), (), s32[]{:S(2)}) async-start(), calls=%async_computation.6 | async-start | bytes 3342336 | tf_op jit(solution)/shard_map/all_gather | solution.py:261
  204.3 3.0 copy-start.5
  204.3 3.0 copy-start.6
  206.9 5.4 %copy-start.1 = (f32[4,8,3072]{2,1,0:T(8,128)}, f32[4,8,3072]{2,1,0:T(8,128)S(1)}, u32[]{:S(2)}) copy-start(f32[4,8,3072]{2,1,0:T(8,128)S(1)} %convert_reduce_fusion.1) | copy-start | bytes 1179652
  212.3 64.7 %all-to-all-start.4 = ((bf16[16,2,8,3072]{3,2,1,0:T(8,128)(2,1)}), bf16[16,2,8,3072]{3,2,1,0:T(8,128)(2,1)}, u32[]{:S(2)}, u32[]{:S(2)}) async-start(bf16[16,2,8,3072]{3,2,1,0:T(8,128)(2,1)} %bitcast.241), calls=%async_computation.4 | async-start | bytes 3145728 | tf_op jit(solution)/shard_map/all_to_all | solution.py:96
  276.9 4.7 %copy-start.25 = (s32[8]{0:T(128)S(1)}, s32[8]{0:T(128)}, u32[]{:S(2)}) copy-start(s32[8]{0:T(128)} %param.21) | copy-start | bytes 100
  276.9 8.3 %copy-start.9 = (f32[8,3072]{1,0:T(8,128)S(1)}, f32[8,3072]{1,0:T(8,128)}, u32[]{:S(2)}) copy-start(f32[8,3072]{1,0:T(8,128)} %get-tuple-element.30) | copy-start | bytes 294916
  276.9 50.9 %all-to-all-start.3 = ((bf16[16,4,8,3072]{3,2,1,0:T(8,128)(2,1)}), bf16[16,4,8,3072]{3,2,1,0:T(8,128)(2,1)}, u32[]{:S(2)}, u32[]{:S(2)}) async-start(bf16[16,4,8,3072]{3,2,1,0:T(8,128)(2,1)} %bitcast.244), calls=%async_computation.3 | async-start | bytes 6291456 | tf_op jit(solution)/shard_map/all_to_all | solution.py:96
  285.2 47.9 %copy-start.13 = (f32[8,2,128]{2,1,0:T(2,128)S(1)}, f32[8,2,128]{2,1,0:T(2,128)}, u32[]{:S(2)}) copy-start(f32[8,2,128]{2,1,0:T(2,128)} %param.20) | copy-start | bytes 24580
  285.2 46.4 %copy-start.7 = (f32[8,3072]{1,0:T(8,128)S(1)}, f32[8,3072]{1,0:T(8,128)}, u32[]{:S(2)}) copy-start(f32[8,3072]{1,0:T(8,128)} %get-tuple-element.71) | copy-start | bytes 294916
  327.8 3.8 %copy-start.8 = (f32[8,3072]{1,0:T(8,128)S(1)}, f32[8,3072]{1,0:T(8,128)}, u32[]{:S(2)}) copy-start(f32[8,3072]{1,0:T(8,128)} %get-tuple-element.72) | copy-start | bytes 294916
  333.1 10.1 %collective-permute-start.15 = (f32[8,1,128]{2,1,0:T(1,128)S(1)}, f32[8,1,128]{2,1,0:T(1,128)S(1)}, u32[]{:S(2)}, u32[]{:S(2)}) collective-permute-start(f32[8,1,128]{2,1,0:T(1,128)S(1)} %get-tuple-element.49), channel_id=1, source_target_pairs={{0,16},{16,32},{32,48},{48,64},{64,80},{80,96},{96,112},{112,128},... | collective-permute-start | bytes 12296 | tf_op jit(solution)/shard_map/ppermute | solution.py:35
  339.4 6.1 %collective-permute-start.16 = (f32[8,1,128]{2,1,0:T(1,128)S(1)}, f32[8,1,128]{2,1,0:T(1,128)S(1)}, u32[]{:S(2)}, u32[]{:S(2)}) collective-permute-start(f32[8,1,128]{2,1,0:T(1,128)S(1)} %get-tuple-element.50), channel_id=1, source_target_pairs={{16,0},{32,16},{48,32},{64,48},{80,64},{96,80},{112,96},{128,112},... | collective-permute-start | bytes 12296 | tf_op jit(solution)/shard_map/ppermute | solution.py:36
Sparse Core Ops, SparseCore 0:
  11.0 64.6 all-gather.2
  208.2 60.8 all-gather.4
